TPU v7x, 512 devices: a whole 4x8x8 slice. The times are simulated.
512 devices in a mesh: seq: 64 (over z, x, core), head: 8 (over y).
Axes of the slice: x: 4, y: 8, z: 8, core: 2. Of those that a mesh axis runs over, the one named last changes fastest.
Arguments:
- projected: float32 [65536, 2560], P(('seq', 'head')), may hold values from -6 to 6
- out_grads: float32 [65536, 2048], P(('seq', 'head')), may hold values from -6 to 6
- conv_weight: float32 [3, 2560], replicated, may hold values from -2.4 to 2.4
- doc_lengths: int32 [16], replicated, may hold values from 1 to 32768, 65536 in all
Outputs:
- grad_projected: float32 [65536, 2560], P(('seq', 'head'))
- grad_conv: float32 [3, 2560], replicated
Inputs may be any that keep to these rules, and one draw needn't show every extreme that they name: `doc_lengths`: the 16 documents fill the 65536 tokens end to end; the longest holds exactly half of 65536 tokens.
All inputs are finite; a program needn't handle non-finite values.
Results may differ from a plain program's by a relative error of at most 0.0003.
Values sent between devices are 32-bit elements; how exact they have to be, the bound alone decides.
No kernel may reach another device: no remote copies, remote signals or barrier semaphores. Data moves between devices by JAX's collectives and lax.ppermute only.
A program may use at most 128 MiB of HBM per device.

v0:
```python
import math
import jax
import jax.numpy as jnp
import numpy as np
from jax import lax
from jax.sharding import PartitionSpec as P

KEY_DIM = 16
HEAD_DIM = 128
HIGHEST = lax.Precision.HIGHEST


def segment_sum(gathered, flags, here, reverse):
    count = gathered.shape[0]
    index = jnp.arange(count, dtype=jnp.int32)
    started = flags > 0.5
    if reverse:
        bound = jnp.min(jnp.where((index > here) & started, index, count - 1))
        take = (index > here) & (index <= bound)
    else:
        bound = jnp.max(jnp.where((index < here) & started, index, 0))
        take = (index >= bound) & (index < here)
    return jnp.sum(jnp.where(take[:, None], gathered, 0.0), axis=0)


def carried_in(state, norm, extra, flags, axis, reverse):
    here = lax.axis_index(axis)
    size = state.size
    packed = jnp.concatenate([state.reshape(-1), norm.reshape(-1), extra])
    width = 128
    padded = jnp.pad(packed, (0, -packed.shape[0] % width)).reshape(-1, width)
    gathered = lax.all_gather(padded, axis).reshape(lax.axis_size(axis), -1)
    if flags is None:
        flags = gathered[:, packed.shape[0] - 1]
    total = segment_sum(gathered[:, : size + norm.size], flags, here, reverse)
    return (total[:size].reshape(state.shape), total[size:].reshape(norm.shape), flags)


def passed_along(value, axis, steps):
    count = lax.axis_size(axis)
    initial, last = (max(0, -steps), min(count, count - steps))
    return lax.ppermute(value, axis, [(source, source + steps) for source in range(initial, last)])


def feature_map(columns):
    key_size = columns.shape[1]
    upper_i, upper_j = np.triu_indices(key_size)
    factors = np.where(upper_i == upper_j, 1.0 / math.sqrt(2.0), 1.0).astype(np.float32)
    products = columns[:, upper_i, :] * columns[:, upper_j, :] * jnp.asarray(factors)[None, :, None]
    constant = jnp.ones((columns.shape[0], 1, columns.shape[2]), jnp.float32)
    return jnp.concatenate([constant, columns, products], axis=1)


def doc_place(doc_lengths, anchor, amount):
    positions = anchor + jnp.arange(amount, dtype=jnp.int32)
    starts = jnp.cumsum(doc_lengths) - doc_lengths
    begins = jnp.max(jnp.where(starts[None, :] <= positions[:, None], starts[None, :], 0), axis=1)
    return (begins, positions - begins)


def conv_forward(signal, leading, weights, offsets):
    row_count = signal.shape[0]
    behind = jnp.concatenate([leading, signal], axis=0)
    back_one = behind[1 : row_count + 1] * (offsets[0:row_count] >= 1).astype(jnp.float32)[:, None]
    back_two = behind[0:row_count] * (offsets[0:row_count] >= 2).astype(jnp.float32)[:, None]
    return weights[0] * signal + weights[1] * back_one + weights[2] * back_two


def conv_backward(grad_rows, trailing, signal, leading, weights, offsets):
    row_count = grad_rows.shape[0]
    ahead_rows = jnp.concatenate([grad_rows, trailing], axis=0)
    ahead_one = (
        ahead_rows[1 : row_count + 1]
        * (offsets[1 : row_count + 1] >= 1).astype(jnp.float32)[:, None]
    )
    ahead_two = (
        ahead_rows[2 : row_count + 2]
        * (offsets[2 : row_count + 2] >= 2).astype(jnp.float32)[:, None]
    )
    grad_signal = weights[0] * grad_rows + weights[1] * ahead_one + weights[2] * ahead_two
    behind = jnp.concatenate([leading, signal], axis=0)
    own_one = (offsets[0:row_count] >= 1).astype(jnp.float32)[:, None]
    own_two = (offsets[0:row_count] >= 2).astype(jnp.float32)[:, None]
    grad_weights = jnp.stack(
        [
            jnp.sum(grad_rows * signal, axis=0),
            jnp.sum(grad_rows * behind[1 : row_count + 1] * own_one, axis=0),
            jnp.sum(grad_rows * behind[0:row_count] * own_two, axis=0),
        ],
        axis=0,
    )
    return (grad_signal, grad_weights)


def attention_grads(mixed_rows, out_flat, begins, stretch_start):
    length = mixed_rows.shape[0]
    head_width = 2 * KEY_DIM + HEAD_DIM
    local_heads = mixed_rows.shape[1] // head_width
    block_len = min(128, length)
    blocks = length // block_len
    scale_key = KEY_DIM ** (-0.25)
    shaped = mixed_rows.reshape(length, local_heads, head_width)
    query_cols = jnp.transpose(shaped[:, :, :KEY_DIM], (1, 2, 0)) * scale_key
    key_cols = jnp.transpose(shaped[:, :, KEY_DIM : 2 * KEY_DIM], (1, 2, 0)) * scale_key
    values = shaped[:, :, 2 * KEY_DIM :]
    upstream = out_flat.reshape(length, local_heads, HEAD_DIM)
    query_feat, query_pull = jax.vjp(feature_map, query_cols)
    key_feat, key_pull = jax.vjp(feature_map, key_cols)
    feat_count = query_feat.shape[1]
    last_begin = begins[length - 1]
    has_start = (last_begin >= stretch_start).astype(jnp.float32).reshape(1)
    tail_mask = (begins == last_begin).astype(jnp.float32)
    tail_feat = key_feat * tail_mask[None, None, :]
    tail_state = jnp.einsum("hfl,lhe->hfe", tail_feat, values, precision=HIGHEST)
    tail_norm = jnp.sum(tail_feat, axis=2)
    prefix = carried_in(tail_state, tail_norm, has_start, None, "seq", False)
    flags = prefix[2]
    causal = jnp.arange(block_len)[:, None] >= jnp.arange(block_len)[None, :]
    indices = jnp.arange(blocks, dtype=jnp.int32)

    def forward_block(carried, block_index):
        carry_state, carry_norm = carried
        offset_rows = block_index * block_len
        block_start = stretch_start + offset_rows
        query_blk = lax.dynamic_slice_in_dim(query_feat, offset_rows, block_len, 2)
        key_blk = lax.dynamic_slice_in_dim(key_feat, offset_rows, block_len, 2)
        value_blk = lax.dynamic_slice_in_dim(values, offset_rows, block_len, 0)
        doc_blk = lax.dynamic_slice_in_dim(begins, offset_rows, block_len, 0)
        allowed = causal & (doc_blk[:, None] == doc_blk[None, :])
        scores = jnp.where(
            allowed[None], jnp.einsum("hft,hfs->hts", query_blk, key_blk, precision=HIGHEST), 0.0
        )
        from_carry = (doc_blk < block_start).astype(jnp.float32)
        numerator = jnp.einsum("hts,she->the", scores, value_blk, precision=HIGHEST) + from_carry[
            :, None, None
        ] * jnp.einsum("hft,hfe->the", query_blk, carry_state, precision=HIGHEST)
        denominator = jnp.sum(scores, axis=2) + from_carry[None, :] * jnp.einsum(
            "hft,hf->ht", query_blk, carry_norm, precision=HIGHEST
        )
        block_tail = (doc_blk == doc_blk[block_len - 1]).astype(jnp.float32)
        carry_keep = (doc_blk[block_len - 1] < block_start).astype(jnp.float32)
        tail_keys = key_blk * block_tail[None, None, :]
        next_state = (
            jnp.einsum("hfs,she->hfe", tail_keys, value_blk, precision=HIGHEST)
            + carry_keep * carry_state
        )
        next_norm = jnp.sum(tail_keys, axis=2) + carry_keep * carry_norm
        return ((next_state, next_norm), (numerator, denominator, carry_state, carry_norm, scores))

    forward_out = lax.scan(forward_block, (prefix[0], prefix[1]), indices)
    numerators, denominators, states, norms, kept_scores = forward_out[1]
    denom_rows = jnp.transpose(denominators, (0, 2, 1)).reshape(length, local_heads)
    attended = numerators.reshape(length, local_heads, HEAD_DIM) / denom_rows[:, :, None]
    grad_num = upstream / denom_rows[:, :, None]
    scalar_grad = -jnp.sum(upstream * attended, axis=2) / denom_rows
    lead_mask = (begins < stretch_start).astype(jnp.float32)
    lead_feat = query_feat * lead_mask[None, None, :]
    lead_state = jnp.einsum("hfl,lhe->hfe", lead_feat, grad_num, precision=HIGHEST)
    lead_norm = jnp.einsum("hfl,lh->hf", lead_feat, scalar_grad, precision=HIGHEST)
    suffix = carried_in(lead_state, lead_norm, jnp.zeros((0,), jnp.float32), flags, "seq", True)

    def backward_block(carried, inputs):
        back_state, back_norm = carried
        block_index, carry_state, carry_norm, scores = inputs
        offset_rows = block_index * block_len
        block_start = stretch_start + offset_rows
        query_blk = lax.dynamic_slice_in_dim(query_feat, offset_rows, block_len, 2)
        key_blk = lax.dynamic_slice_in_dim(key_feat, offset_rows, block_len, 2)
        value_blk = lax.dynamic_slice_in_dim(values, offset_rows, block_len, 0)
        doc_blk = lax.dynamic_slice_in_dim(begins, offset_rows, block_len, 0)
        grad_blk = lax.dynamic_slice_in_dim(grad_num, offset_rows, block_len, 0)
        scalar_blk = lax.dynamic_slice_in_dim(scalar_grad, offset_rows, block_len, 0)
        scalar_cols = scalar_blk.T
        allowed = causal & (doc_blk[:, None] == doc_blk[None, :])
        dscores = jnp.where(
            allowed[None],
            jnp.einsum("the,she->hts", grad_blk, value_blk, precision=HIGHEST)
            + scalar_cols[:, :, None],
            0.0,
        )
        from_carry = (doc_blk < block_start).astype(jnp.float32)
        block_tail = (doc_blk == doc_blk[block_len - 1]).astype(jnp.float32)
        carry_keep = (doc_blk[block_len - 1] < block_start).astype(jnp.float32)
        grad_query = jnp.einsum("hts,hfs->hft", dscores, key_blk, precision=HIGHEST) + from_carry[
            None, None, :
        ] * (
            jnp.einsum("hfe,the->hft", carry_state, grad_blk, precision=HIGHEST)
            + carry_norm[:, :, None] * scalar_cols[:, None, :]
        )
        grad_key = jnp.einsum("hts,hft->hfs", dscores, query_blk, precision=HIGHEST) + block_tail[
            None, None, :
        ] * (
            jnp.einsum("hfe,she->hfs", back_state, value_blk, precision=HIGHEST)
            + back_norm[:, :, None]
        )
        grad_value = jnp.einsum("hts,the->she", scores, grad_blk, precision=HIGHEST) + block_tail[
            :, None, None
        ] * jnp.einsum("hfs,hfe->she", key_blk, back_state, precision=HIGHEST)
        lead_blk = query_blk * from_carry[None, None, :]
        next_state = (
            jnp.einsum("hft,the->hfe", lead_blk, grad_blk, precision=HIGHEST)
            + carry_keep * back_state
        )
        next_norm = (
            jnp.einsum("hft,th->hf", lead_blk, scalar_blk, precision=HIGHEST)
            + carry_keep * back_norm
        )
        return ((next_state, next_norm), (grad_query, grad_key, grad_value))

    swept_back = lax.scan(
        backward_block, (suffix[0], suffix[1]), (indices, states, norms, kept_scores), reverse=True
    )
    grad_qblocks, grad_kblocks, grad_vblocks = swept_back[1]
    query_grad = jnp.transpose(grad_qblocks, (1, 2, 0, 3)).reshape(local_heads, feat_count, length)
    key_grad = jnp.transpose(grad_kblocks, (1, 2, 0, 3)).reshape(local_heads, feat_count, length)
    value_grad = grad_vblocks.reshape(length, local_heads, HEAD_DIM)
    query_in = jnp.transpose(query_pull(query_grad)[0] * scale_key, (2, 0, 1))
    key_in = jnp.transpose(key_pull(key_grad)[0] * scale_key, (2, 0, 1))
    return jnp.concatenate([query_in, key_in, value_grad], axis=2).reshape(
        length, local_heads * head_width
    )


def on_device(projected, out_grads, conv_weight, doc_lengths):
    row_count = projected.shape[0]
    head_count = lax.axis_size("head")
    seq_index = lax.axis_index("seq")
    head_index = lax.axis_index("head")
    group_len = row_count * head_count
    token_base = (seq_index * head_count + head_index) * row_count
    stretch_start = seq_index * group_len
    token_begins, token_offsets = doc_place(doc_lengths, token_base, row_count + 2)
    leading = passed_along(projected[row_count - 2 :], ("seq", "head"), 1)
    outgoing = conv_forward(projected, leading, conv_weight, token_offsets)
    arrived, upstream = (
        lax.all_to_all(outgoing, "head", split_axis=1, concat_axis=0, tiled=True),
        lax.all_to_all(out_grads, "head", split_axis=1, concat_axis=0, tiled=True),
    )
    group_begins, group_offsets = doc_place(doc_lengths, stretch_start, group_len + 2)
    grad_mixed = attention_grads(arrived, upstream, group_begins[:group_len], stretch_start)
    returned = lax.all_to_all(grad_mixed, "head", split_axis=0, concat_axis=1, tiled=True)
    trailing = passed_along(returned[:2], ("seq", "head"), -1)
    grad_projected, weight_part = conv_backward(
        returned, trailing, projected, leading, conv_weight, token_offsets
    )
    grad_conv = lax.psum(weight_part, ("seq", "head"))
    return (grad_projected, grad_conv)


def solution(mesh):
    return jax.shard_map(
        on_device,
        mesh=mesh,
        in_specs=(P(("seq", "head"), None), P(("seq", "head"), None), P(), P()),
        out_specs=(P(("seq", "head"), None), P()),
        check_vma=False,
    )
```

profile of v0, /device:TPU:1, one launch (start us, length us, event | category | flops | bytes accessed | tf_op | source)
XLA Modules:
  0.0 737.0 jit_solution(17403635177316418319)
XLA Ops:
  20.1 6.1 all-to-all-start
  28.1 32.9 %all-to-all-done = f32[128,8,320]{0,2,1:T(8,128)S(1)} async-done(((f32[128,8,320]{0,2,1:T(8,128)}), f32[128,8,320]{0,2,1:T(8,128)S(1)}, u32[]{:S(2)}, u32[]{:S(2)}) %all-to-all-start) | async-done | bytes 1310752 | tf_op jit(solution)/shard_map/all_to_all | solution.py:236
  92.7 28.9 %all-to-all-done.1 = f32[128,8,256]{0,2,1:T(8,128)S(1)} async-done(((f32[128,8,256]{0,2,1:T(8,128)}), f32[128,8,256]{0,2,1:T(8,128)S(1)}, u32[]{:S(2)}, u32[]{:S(2)}) %all-to-all-start.1) | async-done | bytes 1048608 | tf_op jit(solution)/shard_map/all_to_all | solution.py:237
  131.0 48.2 %all-gather.3.cloned.1.call-done = f32[64,309,128]{2,1,0:T(8,128)} async-done(((f32[1,309,128]{2,1,0:T(8,128)}), f32[64,309,128]{2,1,0:T(8,128)}) %all-gather.3.cloned.1.call-update) | async-done | bytes 10125328 | tf_op jit(solution)/shard_map/all_gather | solution.py:32
  179.2 5.7 copy.305
  188.8 110.3 %while.46 = (s32[]{:T(128)}, f32[2,153,128]{2,1,0:T(8,128)S(1)}, f32[2,153]{1,0:T(2,128)S(1)}, f32[8,128,2,128]{1,0,3,2:T(8,128)}, f32[8,2,128]{2,1,0:T(2,128)S(...) while((s32[]{:T(128)}, f32[2,153,128]{2,1,0:T(8,128)S(1)}, ...), condition=%wide.region_10.11_spmd.clone, body=%wide.region_7.10_spmd.clone.sunk | while | flops 231664960 | bytes 3280461 | solution.py:150
  192.8 4.8 dynamic_update_slice.74
  206.6 4.8 dynamic_update_slice.74
  220.4 4.8 dynamic_update_slice.74
  234.2 4.8 dynamic_update_slice.74
  248.0 4.8 dynamic_update_slice.74
  261.8 4.8 dynamic_update_slice.74
  275.6 4.8 dynamic_update_slice.74
  289.3 4.8 dynamic_update_slice.74
  310.3 88.0 %all-gather.5.cloned.1.call-done = f32[64,309,128]{2,1,0:T(8,128)} async-done(((f32[1,309,128]{2,1,0:T(8,128)}), f32[64,309,128]{2,1,0:T(8,128)}) %all-gather.5.cloned.1.call-update) | async-done | bytes 10125328 | tf_op jit(solution)/shard_map/all_gather | solution.py:32
  398.3 5.7 copy.304
  408.5 112.2 %while.47 = (s32[]{:T(128)}, f32[2,153,128]{2,1,0:T(8,128)S(1)}, f32[2,153]{1,0:T(2,128)S(1)}, f32[8,2,153,128]{3,2,1,0:T(8,128)}, f32[8,2,153,128]{3,2,1,0:T(8,...) while((s32[]{:T(128)}, f32[2,153,128]{2,1,0:T(8,128)S(1)}, ...), condition=%wide.region_14.15_spmd.clone, body=%wide.region_13.14_spmd.clone.sunk | while | flops 462717824 | bytes 4866477 | solution.py:210
  529.4 6.0 fusion.85
  535.3 14.0 %scatter_fusion = f32[2,16,1024]{2,0,1:T(2,128)S(1)} fusion(f32[2,16,1024]{2,0,1:T(2,128)S(1)} %split.16, s32[136]{0:T(256)S(1)} %copy-done.16, f32[136,2,1024]{2,1,0:T(2,128)} %get-tuple-element.822), kind=kCustom, calls=%fused_computation.4 | custom fusion | flops 278528 | bytes 3342880 | tf_op jit(solution)/shard_map/transpose(jvp())/scatter-add | solution.py:49
  549.4 7.6 %scatter_fusion.1 = f32[2,16,1024]{2,0,1:T(2,128)S(1)} fusion(f32[2,16,1024]{2,0,1:T(2,128)S(1)} %broadcast.144.clone.1, s32[136]{0:T(256)S(1)} %copy-done.17, f32[136,2,1024]{2,1,0:T(2,128)S(1)} %copy-done.13), kind=kCustom, calls=%fused_computation.5 | custom fusion | flops 278528 | bytes 3342880 | tf_op jit(solution)/shard_map/transpose(jvp())/scatter-add | solution.py:49
  558.4 7.6 %scatter_fusion.3 = f32[2,16,1024]{2,0,1:T(2,128)S(1)} fusion(f32[2,16,1024]{2,0,1:T(2,128)S(1)} %broadcast.144.clone, s32[136]{0:T(256)S(1)} %copy-done.17, f32[136,2,1024]{2,1,0:T(2,128)S(1)} %copy-done.12), kind=kCustom, calls=%fused_computation.7 | custom fusion | flops 278528 | bytes 3342880 | tf_op jit(solution)/shard_map/transpose(jvp())/scatter-add | solution.py:49
  566.0 7.3 scatter_fusion.2
  581.3 41.0 %all_to_all.51 = f32[8,128,320]{1,2,0:T(8,128)S(1)} all-to-all(f32[8,128,320]{1,2,0:T(8,128)S(1)} %copy.248), channel_id=1, replica_groups=mesh['seq'=64,'head'=8] {'head'}, dimensions={0} | all-to-all | bytes 2621440 | tf_op jit(solution)/shard_map/all_to_all | solution.py:241
  626.8 95.7 %psum.7 = f32[3,2560]{1,0:T(4,128)} all-reduce(f32[3,2560]{1,0:T(4,128)S(1)} %pad_maximum_fusion.5), channel_id=1, replica_groups=mesh['seq'=64,'head'=8] {'seq','head'}, use_global_device_ids=true, to_apply=%region_22.23 | all-reduce | flops 7680 | bytes 61440 | tf_op jit(solution)/shard_map/psum | solution.py:246
  (437 shorter events, 266.4 us)
Async XLA Ops:
  8.1 8.5 %collective-permute-start = (f32[2,2560]{1,0:T(2,128)S(1)}, f32[2,2560]{1,0:T(2,128)S(1)}, u32[]{:S(2)}, u32[]{:S(2)}) collective-permute-start(f32[2,2560]{1,0:T(2,128)S(1)} %slice.116), channel_id=1, source_target_pairs={{0,1},{1,2},{2,3},{3,4},{4,5},{5,6},{6,7},{7,8},{8,9},{9,10},{10,1... | collective-permute-start | bytes 61448 | tf_op jit(solution)/shard_map/ppermute | solution.py:42
  16.6 3.5 copy-start.3
  17.0 3.1 copy-start.5
  20.1 7.4 %copy-start.17 = (s32[136]{0:T(256)S(1)}, s32[136]{0:T(256)}, u32[]{:S(2)}) copy-start(s32[136]{0:T(256)} %constant.158) | copy-start | bytes 1636
  20.1 7.4 %copy-start.16 = (s32[136]{0:T(256)S(1)}, s32[136]{0:T(256)}, u32[]{:S(2)}) copy-start(s32[136]{0:T(256)} %constant.159) | copy-start | bytes 1636
  20.1 40.9 %all-to-all-start = ((f32[128,8,320]{0,2,1:T(8,128)}), f32[128,8,320]{0,2,1:T(8,128)S(1)}, u32[]{:S(2)}, u32[]{:S(2)}) async-start(f32[128,8,320]{0,2,1:T(8,128)} %bitcast.248), calls=%async_computation | async-start | bytes 2621440 | tf_op jit(solution)/shard_map/all_to_all | solution.py:236
  26.2 153.0 %all-gather.3.cloned.1.call-start = ((), (), s32[]{:S(2)}) async-start(), calls=%async_computation.3 | async-start | bytes 10383360 | tf_op jit(solution)/shard_map/all_gather | solution.py:32
  26.3 66.3 %copy-start.15 = (s32[1026]{0:T(1024)}, s32[1026]{0:T(1024)S(1)}, u32[]{:S(2)}) copy-start(s32[1026]{0:T(1024)S(1)} %select_reduce_fusion) | copy-start | bytes 12316
  74.2 3.0 copy-start.18
  84.9 2.6 copy-start.14
  88.8 32.7 %all-to-all-start.1 = ((f32[128,8,256]{0,2,1:T(8,128)}), f32[128,8,256]{0,2,1:T(8,128)S(1)}, u32[]{:S(2)}, u32[]{:S(2)}) async-start(f32[128,8,256]{0,2,1:T(8,128)} %bitcast.256), calls=%async_computation.1 | async-start | bytes 2097152 | tf_op jit(solution)/shard_map/all_to_all | solution.py:237
  92.4 305.8 %all-gather.5.cloned.1.call-start = ((), (), s32[]{:S(2)}) async-start(), calls=%async_computation.4 | async-start | bytes 10383360 | tf_op jit(solution)/shard_map/all_gather | solution.py:32
  125.5 1.7 copy-start.10
  126.6 1.4 copy-start.9
  301.4 2.9 copy-start.2
  522.8 1.7 copy-start.8
  526.3 3.1 copy-start.7
  528.3 7.1 copy-start.1
  535.3 14.0 %copy-start.13 = (f32[136,2,1024]{2,1,0:T(2,128)S(1)}, f32[136,2,1024]{2,1,0:T(2,128)}, u32[]{:S(2)}) copy-start(f32[136,2,1024]{2,1,0:T(2,128)} %get-tuple-element.821) | copy-start | bytes 3342340
  558.4 7.6 %slice-start = ((f32[2,153,1024]{2,0,1:T(2,128)}), f32[2,16,1024]{2,0,1:T(2,128)S(1)}, s32[]{:S(2)}) async-start(f32[2,153,1024]{2,0,1:T(2,128)} %copy-done.1), calls=%async_computation.5 | async-start | bytes 262144 | tf_op jit(solution)/shard_map/transpose(jvp())/split | solution.py:51
  558.4 7.6 %copy-start.11 = (f32[136,2,1024]{2,1,0:T(2,128)S(1)}, f32[136,2,1024]{2,1,0:T(2,128)}, u32[]{:S(2)}) copy-start(f32[136,2,1024]{2,1,0:T(2,128)} %get-tuple-element.833) | copy-start | bytes 3342340
  581.3 41.0 %copy-start.4 = (f32[128,2560]{0,1:T(8,128)S(1)}, f32[128,2560]{0,1:T(8,128)}, u32[]{:S(2)}) copy-start(f32[128,2560]{0,1:T(8,128)} %copy-done.3) | copy-start | bytes 3932164
  581.3 41.0 %copy-start.6 = (f32[2,2560]{0,1:T(8,128)S(1)}, f32[2,2560]{0,1:T(8,128)}, u32[]{:S(2)}) copy-start(f32[2,2560]{0,1:T(8,128)} %copy-done.5) | copy-start | bytes 61444
  624.9 97.7 %collective-permute-start.1 = (f32[2,2560]{1,0:T(2,128)S(1)}, f32[2,2560]{1,0:T(2,128)S(1)}, u32[]{:S(2)}, u32[]{:S(2)}) collective-permute-start(f32[2,2560]{1,0:T(2,128)S(1)} %copy.249), channel_id=1, source_target_pairs={{1,0},{2,1},{3,2},{4,3},{5,4},{6,5},{7,6},{8,7},{9,8},{10,9},{11,1... | collective-permute-start | bytes 61448 | tf_op jit(solution)/shard_map/ppermute | solution.py:42
  (3 other events, 3.7 us)
Sparse Core Ops, SparseCore 0:
  87.6 91.5 all-gather.2
  309.7 88.5 all-gather.4
where the time goes:
time: 743 us; the launch traced here: 737 us
  waiting for transfers between devices  198 us (27%)
  local copies, waits for them, and re-layouts  146 us (20%)
  blocking collectives  137 us (18%)
  matrix products  117 us (16%)
  other arithmetic  85.8 us (12%)
  loops' own time  22.4 us (3%)
  starting transfers between devices  15.8 us (2%)
  between operations  15.5 us (2%)
    all_gather x2, waiting for transfers between devices, carried_in(): gathered = lax.all_gather(padded, axis).reshape(lax.axis_size(axis), -1)  136 us
    psum x1, blocking collectives, on_device(): grad_conv = lax.psum(weight_part, ('seq', 'head'))  95.7 us
    dynamic_update_slice x48, local copies, waits for them, and re-layouts, attention_grads(): forward_out = lax.scan(forward_block, (prefix[0], prefix[1]), indices)  55 us
    all_to_all x1, blocking collectives, on_device(): lax.all_to_all(grad_mixed, 'head', split_axis=0, concat_axis=1, tiled=True)  41 us
    all_to_all x1, waiting for transfers between devices, on_device(): lax.all_to_all(outgoing, 'head', split_axis=1, concat_axis=0, tiled=True)  32.9 us
    all_to_all x1, waiting for transfers between devices, on_device(): lax.all_to_all(out_grads, 'head', split_axis=1, concat_axis=0, tiled=True)  28.9 us
    unnamed x48, local copies, waits for them, and re-layouts  23.9 us
    scatter-add x2, other arithmetic, feature_map(): columns[:, upper_j, :]  21.3 us
  transfers between devices with their start and end apart: 6, of which 4 were waited for; matrix products, arithmetic and copies ran while one was open for 2% of the time, Pallas kernels for 0%

commit v1 on v0

--- a/solution.py
+++ b/solution.py
@@ -243,7 +243,7 @@
     grad_projected, weight_part = conv_backward(
         returned, trailing, projected, leading, conv_weight, token_offsets
     )
-    grad_conv = lax.psum(weight_part, ("seq", "head"))
+    grad_conv = lax.psum(lax.psum(weight_part, "seq"), "head")
     return (grad_projected, grad_conv)
 
 

time: 743 us -> 921 us (1.24)
  blocking collectives: 137 us -> 305 us
    psum x1 -> x2, blocking collectives: 95.7 us -> 264 us  [on_device(): grad_conv = lax.psum(lax.psum(weight_part, 'seq'), 'head')]
where the time goes in v1:
time: 921 us; the launch traced here: 907 us
  blocking collectives  305 us (33%)
  waiting for transfers between devices  198 us (21%)
  local copies, waits for them, and re-layouts  146 us (16%)
  matrix products  117 us (13%)
  other arithmetic  85.8 us (9%)
  loops' own time  22.4 us (2%)
  starting transfers between devices  17.9 us (2%)
  between operations  15.5 us (2%)
    psum x2, blocking collectives, on_device(): grad_conv = lax.psum(lax.psum(weight_part, 'seq'), 'head')  264 us
    all_gather x2, waiting for transfers between devices, carried_in(): gathered = lax.all_gather(padded, axis).reshape(lax.axis_size(axis), -1)  136 us
    dynamic_update_slice x48, local copies, waits for them, and re-layouts, attention_grads(): forward_out = lax.scan(forward_block, (prefix[0], prefix[1]), indices)  55 us
    all_to_all x1, blocking collectives, on_device(): lax.all_to_all(grad_mixed, 'head', split_axis=0, concat_axis=1, tiled=True)  41 us
    all_to_all x1, waiting for transfers between devices, on_device(): lax.all_to_all(outgoing, 'head', split_axis=1, concat_axis=0, tiled=True)  32.9 us
    all_to_all x1, waiting for transfers between devices, on_device(): lax.all_to_all(out_grads, 'head', split_axis=1, concat_axis=0, tiled=True)  28.9 us
    unnamed x48, local copies, waits for them, and re-layouts  23.9 us
    scatter-add x2, other arithmetic, feature_map(): columns[:, upper_j, :]  21.3 us
  transfers between devices with their start and end apart: 6, of which 4 were waited for; matrix products, arithmetic and copies ran while one was open for 2% of the time, Pallas kernels for 0%

profile of v1, /device:TPU:1, one launch (start us, length us, event | category | flops | bytes accessed | tf_op | source)
XLA Modules:
  0.0 907.4 jit_solution(11089164403028575608)
XLA Ops:
  20.1 6.1 all-to-all-start
  28.1 32.9 %all-to-all-done = f32[128,8,320]{0,2,1:T(8,128)S(1)} async-done(((f32[128,8,320]{0,2,1:T(8,128)}), f32[128,8,320]{0,2,1:T(8,128)S(1)}, u32[]{:S(2)}, u32[]{:S(2)}) %all-to-all-start) | async-done | bytes 1310752 | tf_op jit(solution)/shard_map/all_to_all | solution.py:236
  92.7 28.9 %all-to-all-done.1 = f32[128,8,256]{0,2,1:T(8,128)S(1)} async-done(((f32[128,8,256]{0,2,1:T(8,128)}), f32[128,8,256]{0,2,1:T(8,128)S(1)}, u32[]{:S(2)}, u32[]{:S(2)}) %all-to-all-start.1) | async-done | bytes 1048608 | tf_op jit(solution)/shard_map/all_to_all | solution.py:237
  131.0 48.2 %all-gather.3.cloned.1.call-done = f32[64,309,128]{2,1,0:T(8,128)} async-done(((f32[1,309,128]{2,1,0:T(8,128)}), f32[64,309,128]{2,1,0:T(8,128)}) %all-gather.3.cloned.1.call-update) | async-done | bytes 10125328 | tf_op jit(solution)/shard_map/all_gather | solution.py:32
  179.2 5.7 copy.305
  188.8 110.3 %while.46 = (s32[]{:T(128)}, f32[2,153,128]{2,1,0:T(8,128)S(1)}, f32[2,153]{1,0:T(2,128)S(1)}, f32[8,128,2,128]{1,0,3,2:T(8,128)}, f32[8,2,128]{2,1,0:T(2,128)S(...) while((s32[]{:T(128)}, f32[2,153,128]{2,1,0:T(8,128)S(1)}, ...), condition=%wide.region_10.11_spmd.clone, body=%wide.region_7.10_spmd.clone.sunk | while | flops 231664960 | bytes 3280461 | solution.py:150
  192.8 4.8 dynamic_update_slice.74
  206.6 4.8 dynamic_update_slice.74
  220.4 4.8 dynamic_update_slice.74
  248.0 4.8 dynamic_update_slice.74
  261.8 4.8 dynamic_update_slice.74
  275.6 4.8 dynamic_update_slice.74
  289.3 4.8 dynamic_update_slice.74
  310.3 88.0 %all-gather.5.cloned.1.call-done = f32[64,309,128]{2,1,0:T(8,128)} async-done(((f32[1,309,128]{2,1,0:T(8,128)}), f32[64,309,128]{2,1,0:T(8,128)}) %all-gather.5.cloned.1.call-update) | async-done | bytes 10125328 | tf_op jit(solution)/shard_map/all_gather | solution.py:32
  398.3 5.7 copy.304
  408.5 112.2 %while.47 = (s32[]{:T(128)}, f32[2,153,128]{2,1,0:T(8,128)S(1)}, f32[2,153]{1,0:T(2,128)S(1)}, f32[8,2,153,128]{3,2,1,0:T(8,128)}, f32[8,2,153,128]{3,2,1,0:T(8,...) while((s32[]{:T(128)}, f32[2,153,128]{2,1,0:T(8,128)S(1)}, ...), condition=%wide.region_14.15_spmd.clone, body=%wide.region_13.14_spmd.clone.sunk | while | flops 462717824 | bytes 4866477 | solution.py:210
  529.4 6.0 fusion.85
  535.3 14.0 %scatter_fusion = f32[2,16,1024]{2,0,1:T(2,128)S(1)} fusion(f32[2,16,1024]{2,0,1:T(2,128)S(1)} %split.16, s32[136]{0:T(256)S(1)} %copy-done.16, f32[136,2,1024]{2,1,0:T(2,128)} %get-tuple-element.822), kind=kCustom, calls=%fused_computation.4 | custom fusion | flops 278528 | bytes 3342880 | tf_op jit(solution)/shard_map/transpose(jvp())/scatter-add | solution.py:49
  549.4 7.6 scatter_fusion.1
  558.4 7.6 scatter_fusion.3
  566.0 7.3 scatter_fusion.2
  581.3 41.0 %all_to_all.51 = f32[8,128,320]{1,2,0:T(8,128)S(1)} all-to-all(f32[8,128,320]{1,2,0:T(8,128)S(1)} %copy.248), channel_id=1, replica_groups=mesh['seq'=64,'head'=8] {'head'}, dimensions={0} | all-to-all | bytes 2621440 | tf_op jit(solution)/shard_map/all_to_all | solution.py:241
  624.5 243.1 %psum.14 = f32[3,2560]{1,0:T(4,128)S(1)} all-reduce(f32[3,2560]{1,0:T(4,128)S(1)} %pad_maximum_fusion.5), channel_id=1, replica_groups=mesh['seq'=64,'head'=8] {'seq'}, use_global_device_ids=true, to_apply=%region_22.23 | all-reduce | flops 7680 | bytes 61440 | tf_op jit(solution)/shard_map/psum | solution.py:246
  871.9 21.0 %psum.15 = f32[3,2560]{1,0:T(4,128)} all-reduce(f32[3,2560]{1,0:T(4,128)S(1)} %psum.14), channel_id=1, replica_groups=mesh['seq'=64,'head'=8] {'head'}, use_global_device_ids=true, to_apply=%region_23.24 | all-reduce | flops 7680 | bytes 61440 | tf_op jit(solution)/shard_map/psum | solution.py:246
  (438 shorter events, 273.3 us)
Async XLA Ops:
  8.1 8.5 collective-permute-start
  16.6 3.5 copy-start.3
  17.0 3.1 copy-start.5
  20.1 7.4 copy-start.17
  20.1 7.4 copy-start.16
  20.1 40.9 %all-to-all-start = ((f32[128,8,320]{0,2,1:T(8,128)}), f32[128,8,320]{0,2,1:T(8,128)S(1)}, u32[]{:S(2)}, u32[]{:S(2)}) async-start(f32[128,8,320]{0,2,1:T(8,128)} %bitcast.248), calls=%async_computation | async-start | bytes 2621440 | tf_op jit(solution)/shard_map/all_to_all | solution.py:236
  26.2 153.0 %all-gather.3.cloned.1.call-start = ((), (), s32[]{:S(2)}) async-start(), calls=%async_computation.3 | async-start | bytes 10383360 | tf_op jit(solution)/shard_map/all_gather | solution.py:32
  26.3 66.3 %copy-start.15 = (s32[1026]{0:T(1024)}, s32[1026]{0:T(1024)S(1)}, u32[]{:S(2)}) copy-start(s32[1026]{0:T(1024)S(1)} %select_reduce_fusion) | copy-start | bytes 12316
  74.2 3.0 copy-start.18
  84.9 2.6 copy-start.14
  88.8 32.7 %all-to-all-start.1 = ((f32[128,8,256]{0,2,1:T(8,128)}), f32[128,8,256]{0,2,1:T(8,128)S(1)}, u32[]{:S(2)}, u32[]{:S(2)}) async-start(f32[128,8,256]{0,2,1:T(8,128)} %bitcast.256), calls=%async_computation.1 | async-start | bytes 2097152 | tf_op jit(solution)/shard_map/all_to_all | solution.py:237
  92.4 305.8 %all-gather.5.cloned.1.call-start = ((), (), s32[]{:S(2)}) async-start(), calls=%async_computation.4 | async-start | bytes 10383360 | tf_op jit(solution)/shard_map/all_gather | solution.py:32
  125.5 1.7 copy-start.10
  126.6 1.4 copy-start.9
  301.4 2.9 copy-start.2
  522.8 1.7 copy-start.8
  526.3 3.1 copy-start.7
  528.3 7.1 copy-start.1
  535.3 14.0 %copy-start.13 = (f32[136,2,1024]{2,1,0:T(2,128)S(1)}, f32[136,2,1024]{2,1,0:T(2,128)}, u32[]{:S(2)}) copy-start(f32[136,2,1024]{2,1,0:T(2,128)} %get-tuple-element.821) | copy-start | bytes 3342340
  558.4 7.6 slice-start
  558.4 7.6 copy-start.11
  581.3 41.0 %copy-start.4 = (f32[128,2560]{0,1:T(8,128)S(1)}, f32[128,2560]{0,1:T(8,128)}, u32[]{:S(2)}) copy-start(f32[128,2560]{0,1:T(8,128)} %copy-done.3) | copy-start | bytes 3932164
  581.3 41.0 %copy-start.6 = (f32[2,2560]{0,1:T(8,128)S(1)}, f32[2,2560]{0,1:T(8,128)}, u32[]{:S(2)}) copy-start(f32[2,2560]{0,1:T(8,128)} %copy-done.5) | copy-start | bytes 61444
  868.0 25.0 %collective-permute-start.1 = (f32[2,2560]{1,0:T(2,128)S(1)}, f32[2,2560]{1,0:T(2,128)S(1)}, u32[]{:S(2)}, u32[]{:S(2)}) collective-permute-start(f32[2,2560]{1,0:T(2,128)S(1)} %copy.249), channel_id=1, source_target_pairs={{1,0},{2,1},{3,2},{4,3},{5,4},{6,5},{7,6},{8,7},{9,8},{10,9},{11,1... | collective-permute-start | bytes 61448 | tf_op jit(solution)/shard_map/ppermute | solution.py:42
  (3 other events, 3.7 us)
Sparse Core Ops, SparseCore 0:
  87.6 91.5 all-gather.2
  309.7 88.5 all-gather.4
